TPU v7x, 32 devices: a whole 2x2x4 slice. The times are simulated.
32 devices in a mesh: sta: 2 (over y), evt: 2 (over core), mode: 8 (over z, x).
Axes of the slice: x: 2, y: 2, z: 4, core: 2. Of those that a mesh axis runs over, the one named last changes fastest.
Arguments:
- receivers: bfloat16 [768, 32768], P('sta', ('mode', 'evt')), may hold values from -6 to 6
- excitations: bfloat16 [32768, 512], P(('mode', 'sta'), 'evt'), may hold values from -0.00390625 to 0.00390625
- mode_freqs: float32 [32768], P('mode'), may hold values from 0 to 1
- mode_damping: float32 [32768], P('mode'), may hold values from 0.02 to 0.2
- sample_freqs: float32 [8], replicated, may hold values from 0.2 to 0.8
Outputs:
- spectra: float32 [768, 2, 8, 512], P(('sta', 'mode'), None, None, 'evt')
All inputs are finite; a program needn't handle non-finite values.
Results may differ from a plain program's by a relative error of at most 0.0029.
Values may be sent and summed in bfloat16 or wider, within the bound.
No kernel may reach another device: no remote copies, remote signals or barrier semaphores. Data moves between devices by JAX's collectives and lax.ppermute only.
A program may use at most 128 MiB of HBM per device.

v0:
```python
import jax
import jax.numpy as jnp
from jax import lax
from jax.sharding import PartitionSpec as P


def resonance(mode_freqs, mode_damping, frequency):
    offset = mode_freqs - frequency
    denominator = offset * offset + mode_damping * mode_damping
    return (mode_damping / denominator, -offset / denominator)


def per_device(receivers, excitations, mode_freqs, mode_damping, sample_freqs):
    receiver_block = lax.all_gather(receivers, "evt", axis=1, tiled=True)
    source_block = lax.all_gather(excitations, "sta", axis=0, tiled=True)
    row_count, mode_count = receiver_block.shape
    real_weight, imag_weight = resonance(
        mode_freqs[None, :], mode_damping[None, :], sample_freqs[:, None]
    )
    weights = jnp.stack([real_weight, imag_weight], axis=0)
    widened = receiver_block.astype(jnp.float32)
    weighted = (widened[:, None, None, :] * weights[None]).astype(jnp.bfloat16)
    partial = jnp.dot(
        weighted.reshape(-1, mode_count), source_block, preferred_element_type=jnp.float32
    )
    partial = partial.reshape(row_count, 2, sample_freqs.shape[0], source_block.shape[1])
    return lax.psum_scatter(partial, "mode", scatter_dimension=0, tiled=True)


def solution(mesh):
    placed = (P("sta", ("mode", "evt")), P(("mode", "sta"), "evt"), P("mode"), P("mode"), P())
    return jax.shard_map(
        per_device,
        mesh=mesh,
        in_specs=placed,
        out_specs=P(("sta", "mode"), None, None, "evt"),
        check_vma=False,
    )
```

profile of v0, /device:TPU:0, one launch (start us, length us, event | category | flops | bytes accessed | tf_op | source)
XLA Modules:
  0.0 204.6 jit_solution(1197653298187763293)
XLA Ops:
  6.5 0.0 all-gather.3.cloned.1.call-start
  6.5 0.7 all-gather.3.cloned.1.call-update
  7.3 0.0 all-gather.5.cloned.1.call-start
  7.3 0.7 all-gather.5.cloned.1.call-update
  8.0 0.0 reduce-scatter.2.cloned.1.call-start
  8.1 0.8 mul.35
  8.9 0.9 fusion.6
  9.7 14.1 %all-gather.3.cloned.1.call-done = bf16[384,4096]{1,0:T(8,128)(2,1)} async-done(((bf16[384,2048]{1,0:T(8,128)(2,1)}), bf16[384,4096]{1,0:T(8,128)(2,1)}) %all-gather.3.cloned.1.call-update) | async-done | bytes 3145744 | tf_op jit(solution)/shard_map/all_gather | solution.py:14
  23.8 5.3 %convert_element_type.8 = f32[384,4096]{1,0:T(8,128)} convert(bf16[384,4096]{1,0:T(8,128)(2,1)} %all-gather.3.cloned.1.call-done) | non-fusion elementwise | flops 1572864 | bytes 9437184 | tf_op jit(solution)/shard_map/convert_element_type | solution.py:21
  29.1 30.5 %all-gather.5.cloned.1.call-done = bf16[4096,256]{1,0:T(8,128)(2,1)} async-done(((bf16[2048,256]{1,0:T(8,128)(2,1)}), bf16[4096,256]{1,0:T(8,128)(2,1)}) %all-gather.5.cloned.1.call-update) | async-done | bytes 2097168 | tf_op jit(solution)/shard_map/all_gather | solution.py:15
  59.7 17.8 %fusion = f32[384,2,8,256]{3,0,2,1:T(8,128)} fusion(f32[2,8,4096]{2,1,0:T(8,128)S(1)} %pad_maximum_fusion, f32[384,4096]{1,0:T(8,128)} %convert_element_type.8, bf16[4096,256]{1,0:T(8,128)(2,1)} %all-gather.5.cloned.1.call-done), kind=kOutput, calls=%fused_computation.1 | convolution fusion | flops 12935233536 | bytes 14942208 | tf_op jit(solution)/shard_map/dot_general | solution.py:23
  77.5 0.0 reduce-scatter.2.cloned.1.call-update
  77.5 118.1 %reduce-scatter.2.cloned.1.call-done = f32[48,2,8,256]{3,0,2,1:T(8,128)} async-done(((f32[384,2,8,256]{3,0,2,1:T(8,128)}), f32[48,2,8,256]{3,0,2,1:T(8,128)}) %reduce-scatter.2.cloned.1.call-update) | async-done | bytes 786448 | tf_op jit(solution)/shard_map/reduce_scatter | solution.py:27
  195.6 2.5 %copy.6 = f32[48,2,8,256]{3,2,1,0:T(8,128)} copy(f32[48,2,8,256]{3,0,2,1:T(8,128)} %reduce-scatter.2.cloned.1.call-done) | data formatting | bytes 1572864 | tf_op jit(solution)/shard_map/reduce_scatter | solution.py:27
  (1 shorter events, 0.0 us)
Async XLA Ops:
  6.5 17.3 %all-gather.3.cloned.1.call-start = ((), (), s32[]{:S(2)}) async-start(), calls=%async_computation.1 | async-start | bytes 4718592 | tf_op jit(solution)/shard_map/all_gather | solution.py:14
  7.3 52.4 %all-gather.5.cloned.1.call-start = ((), (), s32[]{:S(2)}) async-start(), calls=%async_computation.2 | async-start | bytes 3145728 | tf_op jit(solution)/shard_map/all_gather | solution.py:15
  8.0 187.6 %reduce-scatter.2.cloned.1.call-start = ((), (), s32[]{:S(2)}) async-start(), calls=%async_computation.3 | async-start | bytes 7077888 | tf_op jit(solution)/shard_map/reduce_scatter | solution.py:27
Sparse Core Ops, SparseCore 0:
  8.9 14.8 all-gather.2
  25.4 34.2 all-gather.4
  77.7 117.9 reduce-scatter.1
where the time goes:
time: 205 us
  waiting for transfers between devices  164 us (80%)
  matrix products  17.8 us (9%)
  between operations  13.1 us (6%)
  other arithmetic  6.99 us (3%)
  local copies, waits for them, and re-layouts  2.47 us (1%)
    reduce_scatter x1, waiting for transfers between devices, per_device(): return lax.psum_scatter(partial, 'mode', scatter_dimension=0, tiled=True)  118 us
    all_gather x1, waiting for transfers between devices, per_device(): source_block = lax.all_gather(excitations, 'sta', axis=0, tiled=True)  30.5 us
    dot_general x1, matrix products, per_device(): jnp.dot(weighted.reshape(-1, mode_count), source_block, preferred_element...  17.8 us
    all_gather x1, waiting for transfers between devices, per_device(): receiver_block = lax.all_gather(receivers, 'evt', axis=1, tiled=True)  14.1 us
    convert_element_type x1, other arithmetic, per_device(): widened = receiver_block.astype(jnp.float32)  5.32 us
  transfers between devices with their start and end apart: 3, of which 3 were waited for; matrix products, arithmetic and copies ran while one was open for 3% of the time, Pallas kernels for 0%

commit v1 on v0

--- a/solution.py
+++ b/solution.py
@@ -2,6 +2,30 @@
 import jax.numpy as jnp
 from jax import lax
 from jax.sharding import PartitionSpec as P
+
+
+def part_halves_on_mesh(base_x, on_dim):
+    val = list(base_x.shape[1:])
+    val[on_dim] *= base_x.shape[0]
+    return jnp.moveaxis(base_x, 0, on_dim).reshape(val)
+
+
+def tails_name(my_tile, axis_tag):
+    n_dev_all = lax.axis_size(axis_tag)
+    big = my_tile[None]
+    for j in range(n_dev_all.bit_length() - 1):
+        v_now = 1 << j
+        all_values = lax.ppermute(
+            big, axis_name=axis_tag, perm=[(c, c ^ v_now) for c in range(n_dev_all)]
+        )
+        z = jnp.stack([big, all_values])
+        oldest = lax.axis_index(axis_tag) >> j & 1
+        big = jnp.where(oldest == 0, z, z[::-1]).reshape(-1, *my_tile.shape)
+    return big
+
+
+def recover_results_here(block_in, body, array_axis):
+    return part_halves_on_mesh(tails_name(block_in, body), array_axis)
 
 
 def resonance(mode_freqs, mode_damping, frequency):
@@ -12,7 +36,7 @@
 
 def per_device(receivers, excitations, mode_freqs, mode_damping, sample_freqs):
     receiver_block = lax.all_gather(receivers, "evt", axis=1, tiled=True)
-    source_block = lax.all_gather(excitations, "sta", axis=0, tiled=True)
+    source_block = recover_results_here(excitations, "sta", 0)
     row_count, mode_count = receiver_block.shape
     real_weight, imag_weight = resonance(
         mode_freqs[None, :], mode_damping[None, :], sample_freqs[:, None]

time: 205 us -> 183 us (0.89)
  waiting for transfers between devices: 164 us -> 142 us
  starting transfers between devices: 0.08 us -> 3.07 us
    all_gather x1 -> x0, waiting for transfers between devices: 30.5 us -> none  [per_device(): source_block = lax.all_gather(excitations, 'sta', axis=0, tiled=True)]
    ppermute x0 -> x1, waiting for transfers between devices: none -> 21.7 us  [tails_name(): lax.ppermute(big, axis_name=axis_tag, perm=[(c, c ^ v_now) for c in range...]
    all_gather x1, waiting for transfers between devices: 14.1 us -> 0.02 us  [per_device(): receiver_block = lax.all_gather(receivers, 'evt', axis=1, tiled=True)]
    ppermute x0 -> x1, starting transfers between devices: none -> 3.03 us  [tails_name(): lax.ppermute(big, axis_name=axis_tag, perm=[(c, c ^ v_now) for c in range...]
    convert_element_type x1, other arithmetic: 5.32 us -> 2.67 us  [per_device(): widened = receiver_block.astype(jnp.float32)]
  transfers between devices with their start and end apart: 3 -> 3, of which waited for: 3 -> 2; matrix products, arithmetic and copies ran while one was open for 3% -> 1% of each run, Pallas kernels for 0% -> 0%
where the time goes in v1:
time: 183 us; the launch traced here: 182 us
  waiting for transfers between devices  142 us (78%)
  matrix products  16.3 us (9%)
  between operations  13.4 us (7%)
  other arithmetic  5.02 us (3%)
  starting transfers between devices  3.07 us (2%)
  local copies, waits for them, and re-layouts  2.47 us (1%)
    reduce_scatter x1, waiting for transfers between devices, per_device(): return lax.psum_scatter(partial, 'mode', scatter_dimension=0, tiled=True)  120 us
    ppermute x1, waiting for transfers between devices, tails_name(): lax.ppermute(big, axis_name=axis_tag, perm=[(c, c ^ v_now) for c in range...  21.7 us
    dot_general x1, matrix products, per_device(): jnp.dot(weighted.reshape(-1, mode_count), source_block, preferred_element...  16.3 us
  transfers between devices with their start and end apart: 3, of which 2 were waited for; matrix products, arithmetic and copies ran while one was open for 1% of the time, Pallas kernels for 0%

profile of v1, /device:TPU:0, one launch (start us, length us, event | category | flops | bytes accessed | tf_op | source)
XLA Modules:
  0.0 182.4 jit_solution(2598148189016808689)
XLA Ops:
  6.5 0.0 copy-start
  6.5 0.0 all-gather.2.cloned.1.call-start
  6.5 0.7 all-gather.2.cloned.1.call-update
  7.3 0.0 reduce-scatter.2.cloned.1.call-start
  7.3 3.0 %collective-permute-start = (bf16[1,2048,256]{2,1,0:T(8,128)(2,1)}, bf16[1,2048,256]{2,1,0:T(8,128)(2,1)S(1)}, u32[]{:S(2)}, u32[]{:S(2)}) collective-permute-start(bf16[1,2048,256]{2,1,0:T(8,128)(2,1)} %bitcast.10), channel_id=1, source_target_pairs={{0,16},{16,0},{1,17},{17,1},{2,18},{18,2},{3,19},{19,3},{4,20},{20... | collective-permute-start | bytes 3145736 | tf_op jit(solution)/shard_map/ppermute | solution.py:18
  10.3 0.8 mul.35
  11.1 0.9 fusion.5
  12.0 21.7 %collective-permute-done = bf16[1,2048,256]{2,1,0:T(8,128)(2,1)S(1)} collective-permute-done((bf16[1,2048,256]{2,1,0:T(8,128)(2,1)}, bf16[1,2048,256]{2,1,0:T(8,128)(2,1)S(1)}, u32[]{:S(2)}, u32[]{:S(2)}) %collective-permute-start) | collective-permute-done | bytes 1048608 | tf_op jit(solution)/shard_map/ppermute | solution.py:18
  33.7 0.0 copy-done
  33.7 0.2 pad_maximum_fusion
  33.9 0.5 reverse_select_fusion
  34.4 0.0 all-gather.2.cloned.1.call-done
  34.4 2.7 %convert_element_type.8 = f32[384,4096]{1,0:T(8,128)S(1)} convert(bf16[384,4096]{1,0:T(8,128)(2,1)} %all-gather.2.cloned.1.call-done) | non-fusion elementwise | flops 1572864 | bytes 9437184 | tf_op jit(solution)/shard_map/convert_element_type | solution.py:45
  37.1 16.3 %fusion = f32[384,2,8,256]{3,0,2,1:T(8,128)} fusion(bf16[4096,256,1,1]{1,0,3,2:T(8,128)(2,1)S(1)} %bitcast.9, f32[2,8,4096]{2,1,0:T(8,128)S(1)} %pad_maximum_fusion.1, f32[384,4096]{1,0:T(8,128)S(1)} %convert_element_type.8), kind=kOutput, calls=%fused_computation.1 | convolution fusion | flops 12935233536 | bytes 14942208 | tf_op jit(solution)/shard_map/dot_general | solution.py:47
  53.4 0.0 reduce-scatter.2.cloned.1.call-update
  53.4 119.6 %reduce-scatter.2.cloned.1.call-done = f32[48,2,8,256]{3,0,2,1:T(8,128)} async-done(((f32[384,2,8,256]{3,0,2,1:T(8,128)}), f32[48,2,8,256]{3,0,2,1:T(8,128)}) %reduce-scatter.2.cloned.1.call-update) | async-done | bytes 786448 | tf_op jit(solution)/shard_map/reduce_scatter | solution.py:51
  173.0 2.5 %copy.6 = f32[48,2,8,256]{3,2,1,0:T(8,128)} copy(f32[48,2,8,256]{3,0,2,1:T(8,128)} %reduce-scatter.2.cloned.1.call-done) | data formatting | bytes 1572864 | tf_op jit(solution)/shard_map/reduce_scatter | solution.py:51
  (1 shorter events, 0.0 us)
Async XLA Ops:
  6.5 27.2 %copy-start = (bf16[2048,256]{1,0:T(8,128)(2,1)S(1)}, bf16[2048,256]{1,0:T(8,128)(2,1)}, u32[]{:S(2)}) copy-start(bf16[2048,256]{1,0:T(8,128)(2,1)} %param.6) | copy-start | bytes 3145732
  6.5 27.9 %all-gather.2.cloned.1.call-start = ((), (), s32[]{:S(2)}) async-start(), calls=%async_computation.1 | async-start | bytes 4718592 | tf_op jit(solution)/shard_map/all_gather | solution.py:38
  7.3 165.8 %reduce-scatter.2.cloned.1.call-start = ((), (), s32[]{:S(2)}) async-start(), calls=%async_computation.2 | async-start | bytes 7077888 | tf_op jit(solution)/shard_map/reduce_scatter | solution.py:51
  7.3 26.4 %collective-permute-start = (bf16[1,2048,256]{2,1,0:T(8,128)(2,1)}, bf16[1,2048,256]{2,1,0:T(8,128)(2,1)S(1)}, u32[]{:S(2)}, u32[]{:S(2)}) collective-permute-start(bf16[1,2048,256]{2,1,0:T(8,128)(2,1)} %bitcast.10), channel_id=1, source_target_pairs={{0,16},{16,0},{1,17},{17,1},{2,18},{18,2},{3,19},{19,3},{4,20},{20... | collective-permute-start | bytes 3145736 | tf_op jit(solution)/shard_map/ppermute | solution.py:18
Sparse Core Ops, SparseCore 0:
  8.9 14.8 all-gather.1
  53.6 119.4 reduce-scatter.1
